TPU v7x, 512 devices: a whole 4x4x16 slice. The times are simulated.
512 devices in a mesh: lat: 32 (over z, core), lon: 16 (over x, y).
Axes of the slice: x: 4, y: 4, z: 16, core: 2. Of those that a mesh axis runs over, the one named last changes fastest.
Arguments:
- source: float32 [8, 1024, 2048], P(None, 'lat', 'lon'), may hold values from -6 to 6
- kappa_lon: bfloat16 [8, 1024, 2048], P(None, 'lat', 'lon'), may hold values from 32768 to 262144
- kappa_lat: bfloat16 [8, 1024, 2048], P(None, 'lat', 'lon'), may hold values from 2048 to 16384
- sea_mask: int32 [8, 1024, 2048], P(None, 'lat', 'lon'), may hold values 0 or 1
Outputs:
- analysis: float32 [8, 1024, 2048], P(None, 'lat', 'lon')
All inputs are finite; a program needn't handle non-finite values. No bound on the sum of `sea_mask` on one device may be relied on, other than what follows from the above.
Results may differ from a plain program's by a relative error of at most 0.0003.
Values sent between devices are 32-bit elements; how exact they have to be, the bound alone decides.
No kernel may reach another device: no remote copies, remote signals or barrier semaphores. Data moves between devices by JAX's collectives and lax.ppermute only.
A program may use at most 64 MiB of HBM per device.

v0:
```python
import jax
import jax.numpy as jnp
from jax import lax
from jax.sharding import PartitionSpec as P


def earlier(values, stride, axis):
    length = values.shape[axis]
    padding = jnp.zeros_like(lax.slice_in_dim(values, 0, stride, axis=axis))
    return jnp.concatenate([padding, lax.slice_in_dim(values, 0, length - stride, axis=axis)], axis)


def following(values, stride, axis):
    length = values.shape[axis]
    padding = jnp.zeros_like(lax.slice_in_dim(values, 0, stride, axis=axis))
    return jnp.concatenate([lax.slice_in_dim(values, stride, length, axis=axis), padding], axis)


def local_solve(lower_band, upper_band, excess, sources, axis):
    length = lower_band.shape[axis]
    stride = 1
    while stride < length:
        inverse = 1.0 / (excess - lower_band - upper_band)
        left_weight = -lower_band * earlier(inverse, stride, axis)
        right_coefficient = -upper_band * following(inverse, stride, axis)
        new_lower = left_weight * earlier(lower_band, stride, axis)
        new_upper = right_coefficient * following(upper_band, stride, axis)
        excess = (
            excess
            + left_weight * earlier(excess, stride, axis)
            + right_coefficient * following(excess, stride, axis)
        )
        sources = (
            sources
            + left_weight * earlier(sources, stride, axis + 1)
            + right_coefficient * following(sources, stride, axis + 1)
        )
        lower_band, upper_band = (new_lower, new_upper)
        stride = stride * 2
    return sources / (excess - lower_band - upper_band)


def circular_solve(lower_band, upper_band, excess, sources):
    devices = lower_band.shape[0]
    stride = 1
    while stride < devices:
        inverse = 1.0 / (excess - lower_band - upper_band)
        left_weight = -lower_band * jnp.roll(inverse, stride, 0)
        right_coefficient = -upper_band * jnp.roll(inverse, -stride, 0)
        new_lower = left_weight * jnp.roll(lower_band, stride, 0)
        new_upper = right_coefficient * jnp.roll(upper_band, -stride, 0)
        excess = (
            excess
            + left_weight * jnp.roll(excess, stride, 0)
            + right_coefficient * jnp.roll(excess, -stride, 0)
        )
        sources = (
            sources
            + left_weight * jnp.roll(sources, stride, 0)
            + right_coefficient * jnp.roll(sources, -stride, 0)
        )
        lower_band, upper_band = (new_lower, new_upper)
        stride = stride * 2
    return sources / excess


def line_pass(values, faces, edge_kappa, edge_wet, axis, mesh_axis, periodic):
    length = values.shape[axis]
    position = lax.broadcasted_iota(jnp.int32, values.shape, axis)
    zero = jnp.zeros_like(lax.slice_in_dim(values, 0, 1, axis=axis))
    left_face = jnp.concatenate([zero, faces], axis)
    right_face = jnp.concatenate([faces, zero], axis)
    sources = jnp.stack(
        [values, jnp.where(position == 0, 1.0, 0.0), jnp.where(position == length - 1, 1.0, 0.0)], 0
    )
    solved = local_solve(-left_face, -right_face, jnp.ones_like(values), sources, axis)
    particular, from_left, from_right = (solved[0], solved[1], solved[2])

    def row_at(member, place):
        return lax.index_in_dim(member, place, axis, keepdims=False)

    terms = jnp.stack(
        [
            row_at(particular, 0),
            row_at(from_left, 0),
            row_at(from_right, 0),
            row_at(particular, length - 1),
            row_at(from_left, length - 1),
            row_at(from_right, length - 1),
            edge_kappa,
            edge_wet,
        ],
        0,
    )
    gathered = lax.all_gather(terms[None], mesh_axis, axis=0, tiled=True)
    head_p, head_u, head_w, tail_p, tail_u, tail_w, tail_kappa, head_wet = (
        gathered[:, k] for k in range(terms.shape[0])
    )
    devices = gathered.shape[0]

    def next_of(member):
        return jnp.roll(member, -1, 0)

    face = tail_kappa * next_of(head_wet)
    if not periodic:
        device = lax.broadcasted_iota(jnp.int32, face.shape, 0)
        face = jnp.where(device == devices - 1, 0.0, face)
    lower = -face * tail_u
    upper = -face * next_of(head_w)
    diagonal = 1.0 + face * (next_of(head_u) + tail_w)
    flux = circular_solve(lower, upper, diagonal + lower + upper, face * (next_of(head_p) - tail_p))
    index = lax.axis_index(mesh_axis)
    here = lax.dynamic_index_in_dim(flux, index, 0, keepdims=False)
    before = lax.dynamic_index_in_dim(flux, (index + devices - 1) % devices, 0, keepdims=False)
    return (
        particular
        - from_left * jnp.expand_dims(before, axis)
        + from_right * jnp.expand_dims(here, axis)
    )


def shards(source, kappa_lon, kappa_lat, sea_mask):
    wet_cells = sea_mask.astype(jnp.float32)
    lon_kappa = kappa_lon.astype(jnp.float32)
    lat_kappa = kappa_lat.astype(jnp.float32)
    lon_weight = lon_kappa * wet_cells
    lat_weight = lat_kappa * wet_cells
    lon_faces = lon_weight[:, :, :-1] * wet_cells[:, :, 1:]
    lon_pass = line_pass(
        source, lon_faces, lon_weight[:, :, -1], wet_cells[:, :, 0], 2, "lon", True
    )
    lat_faces = lat_weight[:, :-1, :] * wet_cells[:, 1:, :]
    lat_pass = line_pass(
        lon_pass, lat_faces, lat_weight[:, -1, :], wet_cells[:, 0, :], 1, "lat", False
    )
    return wet_cells * 4.0 * jnp.sqrt(jnp.sqrt(lon_kappa * lat_kappa)) * lat_pass


def solution(mesh):
    return jax.shard_map(
        shards,
        mesh=mesh,
        in_specs=(
            P(None, "lat", "lon"),
            P(None, "lat", "lon"),
            P(None, "lat", "lon"),
            P(None, "lat", "lon"),
        ),
        out_specs=P(None, "lat", "lon"),
        check_vma=False,
    )
```

profile of v0, /device:TPU:1, one launch (start us, length us, event | category | flops | bytes accessed | tf_op | source)
XLA Modules:
  0.0 180.2 jit_solution(14112881031736275784)
XLA Ops:
  7.6 1.0 copy.506
  8.6 1.0 copy.505
  9.6 1.2 copy.504
  10.9 0.9 convert_multiply_fusion
  11.9 1.1 slice_negate_fusion.2
  13.0 0.9 subtract_divide_fusion.11
  13.9 0.8 pad_maximum_fusion.1
  14.7 1.5 copy.508
  16.5 0.8 copy-done.2
  17.4 0.9 copy-done.9
  26.4 20.1 %all-gather = f32[128,8,32]{2,1,0:T(8,128)S(1)} all-gather(f32[8,8,32]{2,1,0:T(8,128)S(1)} %constant_dynamic-update-slice_fusion), channel_id=2, replica_groups=mesh['lat'=32,'lon'=16] {'lon'}, dimensions={0}, use_global_device_ids=true | all-gather | bytes 139264 | tf_op jit(solution)/shard_map/all_gather | solution.py:95
  52.8 1.2 slice_multiply_fusion
  54.2 1.3 slice_negate_fusion
  55.5 1.0 subtract_divide_fusion.4
  56.5 1.0 slice.1382
  59.1 1.1 add_divide_fusion.3
  61.8 0.8 copy-done.7
  73.0 0.9 slice_bitcast_fusion
  73.9 1.1 fusion.78
  75.1 1.2 copy.517
  76.3 2.4 %fusion.77 = (f32[8,1,128]{1,0,2:T(8,128)}, f32[8,1,128]{1,0,2:T(8,128)}) fusion(f32[8,32,128]{1,0,2:T(8,128)} %get-tuple-element.112), kind=kLoop, calls=%fused_computation.294 | loop fusion | bytes 16384 | tf_op jit(solution)/shard_map/slice | solution.py:80
  78.7 1.2 copy.518
  79.9 1.1 fusion.76
  81.0 1.3 copy.519
  82.3 1.2 copy.520
  83.5 1.2 copy.521
  84.8 1.2 copy.522
  87.2 78.7 %all-gather.4.cloned.1.call-done = f32[256,8,128]{2,1,0:T(8,128)} async-done(((f32[8,8,128]{2,1,0:T(8,128)}), f32[256,8,128]{2,1,0:T(8,128)}) %all-gather.4.cloned.1.call-update) | async-done | bytes 1048592 | tf_op jit(solution)/shard_map/all_gather | solution.py:95
  166.6 1.1 slice_bitcast_fusion.10
  167.7 1.1 fusion.11
  168.8 1.0 subtract_divide_fusion.16
  172.5 0.9 copy.532
  (286 shorter events, 32.7 us)
Async XLA Ops:
  6.5 159.3 %all-gather.4.cloned.1.call-start = ((), (), s32[]{:S(2)}) async-start(), calls=%async_computation | async-start | bytes 1081344 | tf_op jit(solution)/shard_map/all_gather | solution.py:95
  9.6 2.2 %copy-start.3 = (bf16[8,32,128]{1,0,2:T(8,128)(2,1)}, bf16[8,32,128]{1,0,2:T(8,128)(2,1)S(1)}, u32[]{:S(2)}) copy-start(bf16[8,32,128]{1,0,2:T(8,128)(2,1)S(1)} %copy.505) | copy-start | bytes 196612
  11.8 2.0 %copy-start.5 = (f32[8,32,128]{1,0,2:T(8,128)}, f32[8,32,128]{1,0,2:T(8,128)S(1)}, u32[]{:S(2)}) copy-start(f32[8,32,128]{1,0,2:T(8,128)S(1)} %get-tuple-element.176) | copy-start | bytes 393220
  11.9 2.0 %copy-start.31 = (f32[8,32,128]{2,1,0:T(8,128)S(1)}, f32[8,32,128]{2,1,0:T(8,128)}, u32[]{:S(2)}) copy-start(f32[8,32,128]{2,1,0:T(8,128)} %param.4) | copy-start | bytes 393220
  16.3 1.2 copy-start.19
  17.3 1.2 copy-start.10
  17.3 1.4 copy-start.18
  47.0 5.8 %copy-start.14 = (f32[16,8,32]{2,1,0:T(8,128)}, f32[16,8,32]{2,1,0:T(8,128)S(1)}, u32[]{:S(2)}) copy-start(f32[16,8,32]{2,1,0:T(8,128)S(1)} %get-tuple-element.61) | copy-start | bytes 49156
  47.0 5.8 %copy-start.16 = (f32[16,8,32]{2,1,0:T(8,128)}, f32[16,8,32]{2,1,0:T(8,128)S(1)}, u32[]{:S(2)}) copy-start(f32[16,8,32]{2,1,0:T(8,128)S(1)} %get-tuple-element.62) | copy-start | bytes 49156
  54.0 2.5 %copy-start = (f32[8,32,128]{1,0,2:T(8,128)S(1)}, f32[8,32,128]{1,0,2:T(8,128)}, u32[]{:S(2)}) copy-start(f32[8,32,128]{1,0,2:T(8,128)} %get-tuple-element.175) | copy-start | bytes 393220
  54.1 3.5 %copy-start.15 = (f32[16,8,32]{2,1,0:T(8,128)S(1)}, f32[16,8,32]{2,1,0:T(8,128)}, u32[]{:S(2)}) copy-start(f32[16,8,32]{2,1,0:T(8,128)} %copy-done.14) | copy-start | bytes 49156
  54.1 3.5 %copy-start.17 = (f32[16,8,32]{2,1,0:T(8,128)S(1)}, f32[16,8,32]{2,1,0:T(8,128)}, u32[]{:S(2)}) copy-start(f32[16,8,32]{2,1,0:T(8,128)} %copy-done.16) | copy-start | bytes 49156
  54.1 3.5 %copy-start.22 = (f32[12,8,32]{2,1,0:T(8,128)S(1)}, f32[12,8,32]{2,1,0:T(8,128)}, u32[]{:S(2)}) copy-start(f32[12,8,32]{2,1,0:T(8,128)} %slice.1325) | copy-start | bytes 36868
  54.1 3.5 %copy-start.23 = (f32[12,8,32]{2,1,0:T(8,128)S(1)}, f32[12,8,32]{2,1,0:T(8,128)}, u32[]{:S(2)}) copy-start(f32[12,8,32]{2,1,0:T(8,128)} %slice.1320) | copy-start | bytes 36868
  54.1 3.5 %copy-start.26 = (f32[12,8,32]{2,1,0:T(8,128)S(1)}, f32[12,8,32]{2,1,0:T(8,128)}, u32[]{:S(2)}) copy-start(f32[12,8,32]{2,1,0:T(8,128)} %get-tuple-element.295) | copy-start | bytes 36868
  54.1 3.5 %copy-start.27 = (f32[12,8,32]{2,1,0:T(8,128)S(1)}, f32[12,8,32]{2,1,0:T(8,128)}, u32[]{:S(2)}) copy-start(f32[12,8,32]{2,1,0:T(8,128)} %get-tuple-element.296) | copy-start | bytes 36868
  54.1 3.5 %copy-start.28 = (f32[12,8,32]{2,1,0:T(8,128)S(1)}, f32[12,8,32]{2,1,0:T(8,128)}, u32[]{:S(2)}) copy-start(f32[12,8,32]{2,1,0:T(8,128)} %get-tuple-element.291) | copy-start | bytes 36868
  54.1 3.5 %copy-start.29 = (f32[12,8,32]{2,1,0:T(8,128)S(1)}, f32[12,8,32]{2,1,0:T(8,128)}, u32[]{:S(2)}) copy-start(f32[12,8,32]{2,1,0:T(8,128)} %get-tuple-element.292) | copy-start | bytes 36868
  54.1 3.5 %copy-start.30 = (f32[4,8,32]{2,1,0:T(8,128)S(1)}, f32[4,8,32]{2,1,0:T(8,128)}, u32[]{:S(2)}) copy-start(f32[4,8,32]{2,1,0:T(8,128)} %slice.1319) | copy-start | bytes 12292
  54.1 3.5 %copy-start.34 = (f32[4,8,32]{2,1,0:T(8,128)S(1)}, f32[4,8,32]{2,1,0:T(8,128)}, u32[]{:S(2)}) copy-start(f32[4,8,32]{2,1,0:T(8,128)} %get-tuple-element.293) | copy-start | bytes 12292
  54.2 3.5 %copy-start.35 = (f32[4,8,32]{2,1,0:T(8,128)S(1)}, f32[4,8,32]{2,1,0:T(8,128)}, u32[]{:S(2)}) copy-start(f32[4,8,32]{2,1,0:T(8,128)} %get-tuple-element.294) | copy-start | bytes 12292
  54.2 3.5 %copy-start.36 = (f32[4,8,32]{2,1,0:T(8,128)S(1)}, f32[4,8,32]{2,1,0:T(8,128)}, u32[]{:S(2)}) copy-start(f32[4,8,32]{2,1,0:T(8,128)} %get-tuple-element.289) | copy-start | bytes 12292
  54.2 3.5 %copy-start.37 = (f32[4,8,32]{2,1,0:T(8,128)S(1)}, f32[4,8,32]{2,1,0:T(8,128)}, u32[]{:S(2)}) copy-start(f32[4,8,32]{2,1,0:T(8,128)} %get-tuple-element.290) | copy-start | bytes 12292
  55.5 2.9 %copy-start.24 = (f32[12,8,32]{2,1,0:T(8,128)S(1)}, f32[12,8,32]{2,1,0:T(8,128)}, u32[]{:S(2)}) copy-start(f32[12,8,32]{2,1,0:T(8,128)} %get-tuple-element.275) | copy-start | bytes 36868
  55.5 2.9 %copy-start.25 = (f32[12,8,32]{2,1,0:T(8,128)S(1)}, f32[12,8,32]{2,1,0:T(8,128)}, u32[]{:S(2)}) copy-start(f32[12,8,32]{2,1,0:T(8,128)} %get-tuple-element.276) | copy-start | bytes 36868
  55.5 2.9 %copy-start.32 = (f32[4,8,32]{2,1,0:T(8,128)S(1)}, f32[4,8,32]{2,1,0:T(8,128)}, u32[]{:S(2)}) copy-start(f32[4,8,32]{2,1,0:T(8,128)} %get-tuple-element.277) | copy-start | bytes 12292
  55.5 2.9 %copy-start.33 = (f32[4,8,32]{2,1,0:T(8,128)S(1)}, f32[4,8,32]{2,1,0:T(8,128)}, u32[]{:S(2)}) copy-start(f32[4,8,32]{2,1,0:T(8,128)} %get-tuple-element.278) | copy-start | bytes 12292
  59.1 1.2 copy-start.39
  61.5 1.2 copy-start.8
  61.5 1.4 copy-start.20
  61.5 1.5 copy-start.21
  81.0 5.0 %copy-start.6 = (f32[8,1,128]{1,0,2:T(8,128)S(1)}, f32[8,1,128]{1,0,2:T(8,128)}, u32[]{:S(2)}) copy-start(f32[8,1,128]{1,0,2:T(8,128)} %slice.1382) | copy-start | bytes 12292
  (10 other events, 9.2 us)
Sparse Core Ops, SparseCore 0:
  87.3 78.5 all-gather.3
where the time goes:
time: 181 us; the launch traced here: 180 us
  waiting for transfers between devices  78.7 us (43%)
  local copies, waits for them, and re-layouts  43.2 us (24%)
  other arithmetic  23.2 us (13%)
  blocking collectives  20.1 us (11%)
  between operations  15 us (8%)
    all_gather x1, waiting for transfers between devices, line_pass(): gathered = lax.all_gather(terms[None], mesh_axis, axis=0, tiled=True)  78.7 us
    all_gather x1, blocking collectives, line_pass(): gathered = lax.all_gather(terms[None], mesh_axis, axis=0, tiled=True)  20.1 us
    slice x9, local copies, waits for them, and re-layouts, row_at(): return lax.index_in_dim(member, place, axis, keepdims=False)  12.1 us
    unnamed x99, local copies, waits for them, and re-layouts  9.24 us
    div x12, other arithmetic, local_solve(): inverse = 1.0 / (excess - lower_band - upper_band)  6.03 us
    slice x26, local copies, waits for them, and re-layouts, earlier(): lax.slice_in_dim(values, 0, length - stride, axis=axis)  4.8 us
    add x10, other arithmetic, local_solve(): sources + left_weight * earlier(sources, stride, axis + 1)  4.04 us
  transfers between devices with their start and end apart: 1, of which 1 were waited for; matrix products, arithmetic and copies ran while one was open for 0% of the time, Pallas kernels for 0%

commit v1 on v0

--- a/solution.py
+++ b/solution.py
@@ -92,7 +92,9 @@
         ],
         0,
     )
-    gathered = lax.all_gather(terms[None], mesh_axis, axis=0, tiled=True)
+    gathered = jnp.concatenate(
+        lax.all_to_all(jnp.stack([terms[None]] * lax.axis_size(mesh_axis)), mesh_axis, 0, 0), axis=0
+    )
     head_p, head_u, head_w, tail_p, tail_u, tail_w, tail_kappa, head_wet = (
         gathered[:, k] for k in range(terms.shape[0])
     )

time: 181 us -> 144 us (0.80)
  starting transfers between devices: 0.01 us -> 24 us
  waiting for transfers between devices: 78.7 us -> 55.7 us
  blocking collectives: 20.1 us -> 0 us
  between operations: 15 us -> 1.58 us
  local copies, waits for them, and re-layouts: 43.2 us -> 39.3 us
    all_gather x1 -> x0, waiting for transfers between devices: 78.7 us -> none  [line_pass(): gathered = lax.all_gather(terms[None], mesh_axis, axis=0, tiled=True)]
    all_to_all x0 -> x2, waiting for transfers between devices: none -> 55.7 us  [line_pass(): lax.all_to_all(jnp.stack([terms[None]] * lax.axis_size(mesh_axis)), mesh_...]
    all_to_all x0 -> x2, starting transfers between devices: none -> 24 us  [line_pass(): lax.all_to_all(jnp.stack([terms[None]] * lax.axis_size(mesh_axis)), mesh_...]
    all_gather x1 -> x0, blocking collectives: 20.1 us -> none  [line_pass(): gathered = lax.all_gather(terms[None], mesh_axis, axis=0, tiled=True)]
    unnamed x99 -> x69, local copies, waits for them, and re-layouts: 9.24 us -> 13.1 us
    slice x9, local copies, waits for them, and re-layouts: 12.1 us -> 8.9 us  [row_at(): return lax.index_in_dim(member, place, axis, keepdims=False)]
    div x12, other arithmetic: 6.03 us -> 8.79 us  [local_solve(): inverse = 1.0 / (excess - lower_band - upper_band)]
    another operation x0 -> x2, local copies, waits for them, and re-layouts: none -> 1.99 us  [line_pass(): jnp.stack([terms[None]] * lax.axis_size(mesh_axis))]
  transfers between devices with their start and end apart: 1 -> 2, of which waited for: 1 -> 1; matrix products, arithmetic and copies ran while one was open for 0% -> 9% of each run, Pallas kernels for 0% -> 0%
where the time goes in v1:
time: 144 us; the launch traced here: 143 us
  waiting for transfers between devices  55.7 us (39%)
  local copies, waits for them, and re-layouts  39.3 us (27%)
  starting transfers between devices  24 us (17%)
  other arithmetic  22 us (15%)
  between operations  1.58 us (1%)
    all_to_all x2, waiting for transfers between devices, line_pass(): lax.all_to_all(jnp.stack([terms[None]] * lax.axis_size(mesh_axis)), mesh_...  55.7 us
    all_to_all x2, starting transfers between devices, line_pass(): lax.all_to_all(jnp.stack([terms[None]] * lax.axis_size(mesh_axis)), mesh_...  24 us
    unnamed x69, local copies, waits for them, and re-layouts  13.1 us
    slice x9, local copies, waits for them, and re-layouts, row_at(): return lax.index_in_dim(member, place, axis, keepdims=False)  8.9 us
    div x12, other arithmetic, local_solve(): inverse = 1.0 / (excess - lower_band - upper_band)  8.79 us
    slice x26, local copies, waits for them, and re-layouts, earlier(): lax.slice_in_dim(values, 0, length - stride, axis=axis)  4.8 us
    add x10, other arithmetic, local_solve(): sources + left_weight * earlier(sources, stride, axis + 1)  4.06 us
  transfers between devices with their start and end apart: 2, of which 1 were waited for; matrix products, arithmetic and copies ran while one was open for 9% of the time, Pallas kernels for 0%

profile of v1, /device:TPU:1, one launch (start us, length us, event | category | flops | bytes accessed | tf_op | source)
XLA Modules:
  0.0 142.6 jit_solution(13016574147526797801)
XLA Ops:
  0.0 1.0 copy.395
  1.0 1.0 copy.394
  2.1 1.2 copy.393
  3.4 0.9 convert_multiply_fusion
  4.3 1.0 slice_negate_fusion.2
  5.4 0.9 subtract_divide_fusion.11
  7.1 1.5 %copy.397 = f32[3,8,32,128]{2,1,3,0:T(8,128)S(1)} copy(f32[3,8,32,128]{3,2,1,0:T(8,128)} %pad_maximum_fusion.1) | data formatting | bytes 786432 | tf_op jit(solution)/shard_map/stack | solution.py:73
  8.9 0.8 copy-done.1
  9.8 0.9 copy-done.18
  18.8 0.9 stack.34
  19.7 1.9 %reshape.62 = f32[16,1,2048]{2,1,0:T(1,128)} reshape(f32[16,1,8,8,32]{4,3,2,1,0:T(8,128)} %stack.34) | data formatting | bytes 262144
  21.6 7.8 %all-to-all-start = ((f32[16,1,2048]{2,1,0:T(1,128)}), f32[16,1,2048]{2,1,0:T(1,128)S(1)}, u32[]{:S(2)}, u32[]{:S(2)}) async-start(f32[16,1,2048]{2,1,0:T(1,128)} %reshape.62), calls=%async_computation | async-start | bytes 262144 | tf_op jit(solution)/shard_map/all_to_all | solution.py:96
  31.1 1.4 subtract_divide_fusion.3
  33.1 1.4 %subtract_divide_fusion.2 = (f32[8,32,128]{1,0,2:T(8,128)S(1)}, f32[8,32,128]{1,0,2:T(8,128)S(1)}, f32[8,32,128]{1,0,2:T(8,128)S(1)}, f32[8,32,128]{1,0,2:T(8,12...) fusion(f32[8,30,128]{1,0,2:T(8,128)S(1)} %bitcast.192, f32[8,30,128]{1,0,2:T(8,128)S(1)} %get-tuple-element.315, ...), kind=kLoop, calls=%fused_computation.42 | loop fusion | flops 425984 | bytes 1916928 | tf_op jit(solution)/shard_map/div | solution.py:23
  35.1 1.4 subtract_divide_fusion.1
  37.1 1.5 %subtract_divide_fusion = (f32[8,32,128]{1,0,2:T(8,128)S(1)}, f32[8,32,128]{1,0,2:T(8,128)S(1)}, f32[8,32,128]{1,0,2:T(8,128)S(1)}, f32[8,32,128]{1,0,2:T(8,128)...) fusion(f32[8,24,128]{1,0,2:T(8,128)S(1)} %bitcast.194, f32[8,24,128]{1,0,2:T(8,128)S(1)} %get-tuple-element.162, ...), kind=kLoop, calls=%fused_computation.30 | loop fusion | flops 425984 | bytes 1769472 | tf_op jit(solution)/shard_map/div | solution.py:23
  39.2 1.6 %multiply_subtract_fusion = (f32[8,32,128]{1,0,2:T(8,128)}, f32[8,32,128]{1,0,2:T(8,128)}, f32[8,32,128]{1,0,2:T(8,128)}) fusion(f32[8,16,128]{1,0,2:T(8,128)S(1)} %slice.1372, f32[8,16,128]{1,0,2:T(8,128)S(1)} %bitcast.191, f32[8,16,128]{1,0,2:T(8,128)S(1)} %get-tuple-element.158, f32[8,32,128]{1,0,2:T(8,128)S(1)} %get-tuple-element.32, ...), kind=kLoop, calls=%fused_computation.27 | loop fusion | flops 393216 | bytes 1179648 | tf_op jit(solution)/shard_map/sub | solution.py:40
  40.8 1.0 slice.1382
  41.9 1.2 copy.412
  43.9 0.9 reduce
  55.5 1.1 fusion.78
  56.6 1.2 copy.406
  57.8 1.1 fusion.77
  59.0 1.3 copy.407
  60.3 1.2 fusion.76
  61.4 1.3 copy.408
  62.9 1.2 copy.410
  64.5 1.1 stack.38
  65.6 16.3 %all-to-all-start.1 = ((f32[32,1,8,8,128]{4,3,2,1,0:T(8,128)}), f32[32,1,8,8,128]{4,3,2,1,0:T(8,128)}, u32[]{:S(2)}, u32[]{:S(2)}) async-start(f32[32,1,8,8,128]{4,3,2,1,0:T(8,128)} %stack.38), calls=%async_computation.1 | async-start | bytes 2097152 | tf_op jit(solution)/shard_map/all_to_all | solution.py:96
  81.9 55.7 %all-to-all-done.1 = f32[32,1,8,8,128]{4,3,2,1,0:T(8,128)} async-done(((f32[32,1,8,8,128]{4,3,2,1,0:T(8,128)}), f32[32,1,8,8,128]{4,3,2,1,0:T(8,128)}, u32[]{:S(2)}, u32[]{:S(2)}) %all-to-all-start.1) | async-done | bytes 1048608 | tf_op jit(solution)/shard_map/all_to_all | solution.py:96
  137.6 1.3 copy.426
  141.8 0.9 copy.417
  (261 shorter events, 26.9 us)
Async XLA Ops:
  2.1 2.2 %copy-start.2 = (bf16[8,32,128]{1,0,2:T(8,128)(2,1)}, bf16[8,32,128]{1,0,2:T(8,128)(2,1)S(1)}, u32[]{:S(2)}) copy-start(bf16[8,32,128]{1,0,2:T(8,128)(2,1)S(1)} %copy.394) | copy-start | bytes 196612
  4.3 2.0 %copy-start.6 = (f32[8,32,128]{1,0,2:T(8,128)}, f32[8,32,128]{1,0,2:T(8,128)S(1)}, u32[]{:S(2)}) copy-start(f32[8,32,128]{1,0,2:T(8,128)S(1)} %get-tuple-element.176) | copy-start | bytes 393220
  4.3 2.0 %copy-start.24 = (f32[8,32,128]{2,1,0:T(8,128)S(1)}, f32[8,32,128]{2,1,0:T(8,128)}, u32[]{:S(2)}) copy-start(f32[8,32,128]{2,1,0:T(8,128)} %param.4) | copy-start | bytes 393220
  8.6 1.0 copy-start.1
  8.6 1.2 copy-start.21
  9.7 1.1 copy-start.18
  9.7 1.2 copy-start.19
  9.7 1.4 copy-start.20
  17.9 11.4 %copy-start = (f32[8,32,128]{1,0,2:T(8,128)S(1)}, f32[8,32,128]{1,0,2:T(8,128)}, u32[]{:S(2)}) copy-start(f32[8,32,128]{1,0,2:T(8,128)} %get-tuple-element.175) | copy-start | bytes 393220
  21.6 21.7 %all-to-all-start = ((f32[16,1,2048]{2,1,0:T(1,128)}), f32[16,1,2048]{2,1,0:T(1,128)S(1)}, u32[]{:S(2)}, u32[]{:S(2)}) async-start(f32[16,1,2048]{2,1,0:T(1,128)} %reshape.62), calls=%async_computation | async-start | bytes 262144 | tf_op jit(solution)/shard_map/all_to_all | solution.py:96
  29.9 1.0 copy-start.22
  29.9 1.2 copy-start.23
  46.3 1.0 copy-start.4
  46.3 1.2 copy-start.5
  48.0 1.0 copy-start.9
  48.0 1.2 copy-start.10
  49.7 1.0 copy-start.11
  49.7 1.2 copy-start.12
  51.5 1.0 copy-start.13
  51.5 1.2 copy-start.14
  53.2 1.0 copy-start.15
  53.2 1.2 copy-start.16
  53.2 1.3 copy-start.17
  59.0 3.7 %copy-start.7 = (f32[8,1,128]{1,0,2:T(8,128)S(1)}, f32[8,1,128]{1,0,2:T(8,128)}, u32[]{:S(2)}) copy-start(f32[8,1,128]{1,0,2:T(8,128)} %get-tuple-element.153) | copy-start | bytes 12292
  61.4 2.8 %copy-start.8 = (f32[8,1,128]{1,0,2:T(8,128)S(1)}, f32[8,1,128]{1,0,2:T(8,128)}, u32[]{:S(2)}) copy-start(f32[8,1,128]{1,0,2:T(8,128)} %get-tuple-element.149) | copy-start | bytes 12292
  65.6 72.0 %all-to-all-start.1 = ((f32[32,1,8,8,128]{4,3,2,1,0:T(8,128)}), f32[32,1,8,8,128]{4,3,2,1,0:T(8,128)}, u32[]{:S(2)}, u32[]{:S(2)}) async-start(f32[32,1,8,8,128]{4,3,2,1,0:T(8,128)} %stack.38), calls=%async_computation.1 | async-start | bytes 2097152 | tf_op jit(solution)/shard_map/all_to_all | solution.py:96
  140.4 1.0 copy-start.3
